TPU v7x, 128 devices: a whole 4x4x4 slice. The times are simulated.
128 devices in a mesh: row: 16 (over x, y), col: 8 (over z, core).
Axes of the slice: x: 4, y: 4, z: 4, core: 2. Of those that a mesh axis runs over, the one named last changes fastest.
Arguments:
- pattern_in: int32 [64, 16], replicated, may hold values from 0 to 63, as said below
- pattern_mid: int32 [64, 16], replicated, may hold values from 0 to 63, as said below
- pattern_out: int32 [64, 16], replicated, may hold values from 0 to 63, as said below
- density_blocks: float32 [4, 16, 2, 8, 256, 256], P(None, 'row', None, 'col'), as said below
Outputs:
- purified_blocks: float32 [4, 16, 2, 8, 256, 256], P(None, 'row', None, 'col')
Inputs may be any that keep to these rules, and one draw needn't show every extreme that they name: `pattern_in`: slot l * 8 + c of block row I names a block column congruent to c modulo 8; no column stands twice in a row; slot I mod 8 of row I names I; J stands in row I exactly when I stands in row J. `pattern_mid`: as for pattern_in. `pattern_out`: as for pattern_in. `density_blocks`: the block of row J for column I is the transpose of the block of row I for column J.
All inputs are finite; a program needn't handle non-finite values.
Results may differ from a plain program's by a relative error of at most 0.0091.
Values may be sent and summed in bfloat16 or wider, within the bound.
No kernel may reach another device: no remote copies, remote signals or barrier semaphores. Data moves between devices by JAX's collectives and lax.ppermute only.
A program may use at most 128 MiB of HBM per device.

v0:
```python
import jax
import jax.numpy as jnp
from jax import lax
from jax.sharding import PartitionSpec as P

ITERS = 2


def purify_section(owned, cur_list, next_list, grid_rows, grid_cols, row_index, col_index):
    block_rows = owned.shape[0]
    slot_pairs = owned.shape[2]
    edge_size = owned.shape[4]
    total_rows = cur_list.shape[0]
    slot_count = cur_list.shape[1]
    occupied = total_rows * edge_size / 2.0
    panels = owned.astype(jnp.bfloat16)
    owned_slots = owned[:, 0, :, 0]
    my_rows = lax.dynamic_index_in_dim(
        cur_list.reshape(block_rows, grid_rows, slot_count), row_index, axis=1, keepdims=False
    )
    my_residue = lax.dynamic_index_in_dim(
        my_rows.reshape(block_rows, slot_pairs, grid_cols), col_index, axis=2, keepdims=False
    )
    own_index = jnp.arange(block_rows, dtype=jnp.int32) * grid_rows + row_index
    diag_term = jnp.sum(
        jnp.where(my_residue == own_index[:, None], jnp.trace(owned_slots, axis1=2, axis2=3), 0.0)
    )
    next_trace = None
    trace_now = lax.psum(diag_term, ("row", "col"))
    gathered_rows = lax.all_gather(panels, "col", axis=3, tiled=True).reshape(
        block_rows, slot_count, edge_size, edge_size
    )
    next_rows = lax.dynamic_index_in_dim(
        next_list.reshape(block_rows, grid_rows, slot_count), row_index, axis=1, keepdims=False
    )
    out_cols = lax.dynamic_index_in_dim(
        next_rows.reshape(block_rows, slot_pairs, grid_cols), col_index, axis=2, keepdims=False
    )
    inner_safe = jnp.maximum(my_rows, 0)
    valid_inner = my_rows >= 0
    valid_out = out_cols >= 0
    column_panels = lax.all_gather(panels, "row", axis=1, tiled=True).reshape(
        total_rows * slot_pairs, edge_size, edge_size
    )
    residue_lists = lax.dynamic_index_in_dim(
        cur_list.reshape(total_rows, slot_pairs, grid_cols), col_index, axis=2, keepdims=False
    )
    candidates = residue_lists[inner_safe]
    matches = (
        (candidates[:, None, :, :] == out_cols[:, :, None, None])
        & valid_inner[:, None, :, None]
        & valid_out[:, :, None, None]
    )
    chosen = jnp.sum(matches * jnp.arange(slot_pairs, dtype=jnp.int32), axis=-1)
    present = jnp.any(matches, axis=-1)
    position = inner_safe[:, None, :] * slot_pairs + chosen
    picked = jnp.where(
        present[..., None, None], column_panels[position], jnp.zeros((), jnp.bfloat16)
    )
    product = jnp.einsum(
        "ikuv,ilkvw->iluw", gathered_rows, picked, preferred_element_type=jnp.float32
    )
    keep = (my_residue[:, None, :] == out_cols[:, :, None]) & valid_out[:, :, None]
    previous = jnp.sum(jnp.where(keep[..., None, None], owned_slots[:, None], 0.0), axis=2)
    updated = jnp.where(trace_now > occupied, product, 2.0 * previous - product)
    return (updated.reshape(block_rows, 1, slot_pairs, 1, edge_size, edge_size), next_trace)


def shards(pattern_in, pattern_mid, pattern_out, density_blocks):
    grid_rows = lax.axis_size("row")
    grid_cols = lax.axis_size("col")
    row_index = lax.axis_index("row")
    col_index = lax.axis_index("col")
    all_lists = (pattern_in, pattern_mid, pattern_out)
    current = density_blocks
    for iteration in range(ITERS):
        current, known_trace = purify_section(
            current,
            all_lists[iteration],
            all_lists[iteration + 1],
            grid_rows,
            grid_cols,
            row_index,
            col_index,
        )
    return current


def solution(mesh):
    in_specs = (P(), P(), P(), P(None, "row", None, "col", None, None))
    out_specs = P(None, "row", None, "col", None, None)
    return jax.shard_map(shards, mesh=mesh, in_specs=in_specs, out_specs=out_specs, check_vma=False)
```

profile of v0, /device:TPU:1, one launch (start us, length us, event | category | flops | bytes accessed | tf_op | source)
XLA Modules:
  0.0 392.0 jit_solution(4681731561013483844)
XLA Ops:
  6.5 2.8 convert_element_type.11
  9.5 0.7 all-gather.9.cloned.1.call-update
  10.2 1.8 copy.96
  12.2 0.1 copy.128
  12.5 0.1 copy.94
  12.7 1.9 fusion.9
  14.6 0.7 select_reduce_fusion.6
  15.3 72.1 %psum.14 = f32[]{:T(128)} all-reduce(f32[]{:T(128)} %select_reduce_fusion.6), channel_id=1, replica_groups=mesh['row'=16,'col'=8] {'row','col'}, use_global_device_ids=true, to_apply=%region_2.3 | all-reduce | flops 1 | bytes 8 | tf_op jit(solution)/shard_map/psum | solution.py:29
  87.6 0.1 copy.127
  87.8 0.2 compare_reduce_fusion.1
  88.3 0.1 copy.131
  88.5 0.2 compare_reduce_fusion
  89.0 0.6 gather_fusion
  90.2 1.7 select_reduce_fusion.1
  92.0 2.0 copy.106
  94.6 30.6 %all-gather.7.cloned.1.call-done = bf16[4,16,2,1,256,256]{5,4,3,2,1,0:T(8,128)(2,1)} async-done(((bf16[4,1,2,1,256,256]{5,4,3,2,1,0:T(8,128)(2,1)}), bf16[4,16,2,1,256,256]{5,4,3,2,1,0:T(8,128)(2,1)}) %all-gather.7.cloned.1.call-update) | async-done | bytes 16777232 | tf_op jit(solution)/shard_map/all_gather | solution.py:42
  125.2 14.7 %gather_fusion.1 = bf16[128,256,256]{2,1,0:T(8,128)(2,1)} fusion(bf16[128,256,256]{2,1,0:T(8,128)(2,1)} %bitcast.85, s32[1024]{0:T(1024)S(1)} %pad_clamp_fusion.2), kind=kCustom, calls=%fused_computation.1 | custom fusion | bytes 33554944 | tf_op jit(solution)/shard_map/gather | solution.py:58
  139.8 21.8 %copy.102 = bf16[128,256,256]{1,2,0:T(8,128)(2,1)} copy(bf16[128,256,256]{2,1,0:T(8,128)(2,1)} %gather_fusion.1) | data formatting | bytes 33554432 | tf_op jit(solution)/shard_map/gather | solution.py:58
  161.6 15.0 %all-gather.9.cloned.1.call-done = bf16[4,1,2,8,256,256]{5,4,3,2,1,0:T(8,128)(2,1)} async-done(((bf16[4,1,2,1,256,256]{5,4,3,2,1,0:T(8,128)(2,1)}), bf16[4,1,2,8,256,256]{5,4,3,2,1,0:T(8,128)(2,1)}) %all-gather.9.cloned.1.call-update) | async-done | bytes 8388624 | tf_op jit(solution)/shard_map/all_gather | solution.py:30
  176.6 12.1 %select_reduce_fusion.2 = (f32[4,2]{1,0:T(4,128)S(1)}, bf16[4,2,256,256]{2,3,1,0:T(8,128)(2,1)}, f32[4,2,256,256]{2,3,1,0:T(8,128)}) fusion(pred[256,256]{0,1:T(8,128)(4,1)S(1)} %iota_compare_fusion, f32[4,2,256,256]{2,3,1,0:T(8,128)S(1)} %copy.106, bf16[4,16,256,256,1]{3,2,1,4,0:T(8,128)(2,1)} %bitcast.101, bf16[4,2,16,256,256]{3,4,2,1,0:T(8,128)(2,1)} %bitcast.87, ...), kind=kOutput, calls=%fused_computation.19 | convolution fusion | flops 4306501632 | bytes 30474400 | tf_op jit(solution)/shard_map/ikuv,ilkvw->iluw/dot_general | solution.py:60
  188.8 0.5 all-gather.11.cloned.1.call-update
  189.5 0.6 gather_fusion.2
  190.5 0.8 select_reduce_fusion.5
  191.2 66.4 %psum.15 = f32[]{:T(128)} all-reduce(f32[]{:T(128)} %select_reduce_fusion.5), channel_id=1, replica_groups=mesh['row'=16,'col'=8] {'row','col'}, use_global_device_ids=true, to_apply=%region_8.9 | all-reduce | flops 1 | bytes 8 | tf_op jit(solution)/shard_map/psum | solution.py:29
  257.6 2.2 copy.117
  259.8 1.7 select_reduce_fusion
  261.5 1.9 copy.118
  264.2 11.5 %copy.114 = bf16[4,2,2048,256]{3,2,1,0:T(8,128)(2,1)} copy(bf16[4,2,2048,256]{2,3,1,0:T(8,128)(2,1)} %all-gather.13.cloned.1.call-done) | data formatting | bytes 16777216 | tf_op jit(solution)/shard_map/all_gather | solution.py:30
  275.7 81.2 %all-gather.11.cloned.1.call-done = bf16[4,32,256,256]{2,3,1,0:T(8,128)(2,1)} async-done(((bf16[4,2,256,256]{2,3,1,0:T(8,128)(2,1)}), bf16[4,32,256,256]{2,3,1,0:T(8,128)(2,1)}) %all-gather.11.cloned.1.call-update) | async-done | bytes 16777232 | tf_op jit(solution)/shard_map/all_gather | solution.py:42
  356.9 14.1 %gather_fusion.3 = bf16[128,256,256]{1,2,0:T(8,128)(2,1)} fusion(bf16[128,256,256]{1,2,0:T(8,128)(2,1)} %bitcast.86, s32[1024]{0:T(1024)S(1)} %pad_clamp_fusion), kind=kCustom, calls=%fused_computation.3 | custom fusion | bytes 33554944 | tf_op jit(solution)/shard_map/gather | solution.py:58
  371.0 11.6 %fusion.8 = f32[4,1,2,1,256,256]{4,5,2,0,3,1:T(8,128)} fusion(f32[4,2,256,256]{2,3,1,0:T(8,128)S(1)} %copy.118, bf16[4,16,256,256,1]{3,2,1,4,0:T(8,128)(2,1)} %bitcast.89, bf16[4,2,16,256,256]{3,4,2,1,0:T(8,128)(2,1)} %bitcast.88, pred[4,2,16]{2,1,0:T(4,128)(4,1)S(1)} %copy.112, pred[]{:T(512)S(6)} %gt.7), kind=kOutput, calls=%fused_computation.16 | convolution fusion | flops 4304928768 | bytes 29360256 | tf_op jit(solution)/shard_map/ikuv,ilkvw->iluw/dot_general | solution.py:60
  382.5 2.9 copy.119
  (57 shorter events, 2.6 us)
Async XLA Ops:
  6.5 3.7 copy-start
  6.5 5.5 %copy-start.2 = (s32[64,16]{0,1:T(8,128)S(1)}, s32[64,16]{0,1:T(8,128)}, u32[]{:S(2)}) copy-start(s32[64,16]{0,1:T(8,128)} %param.4) | copy-start | bytes 12292
  6.5 118.6 %all-gather.7.cloned.1.call-start = ((), (), s32[]{:S(2)}) async-start(), calls=%async_computation | async-start | bytes 17825792 | tf_op jit(solution)/shard_map/all_gather | solution.py:42
  9.4 78.1 %copy-start.1 = (s32[64,16]{0,1:T(8,128)S(1)}, s32[64,16]{0,1:T(8,128)}, u32[]{:S(2)}) copy-start(s32[64,16]{0,1:T(8,128)} %param.5) | copy-start | bytes 12292
  9.4 78.8 %copy-start.3 = (s32[64,16]{0,1:T(8,128)S(1)}, s32[64,16]{0,1:T(8,128)}, u32[]{:S(2)}) copy-start(s32[64,16]{0,1:T(8,128)} %param.6) | copy-start | bytes 12292
  9.4 167.2 %all-gather.9.cloned.1.call-start = ((), (), s32[]{:S(2)}) async-start(), calls=%async_computation.1 | async-start | bytes 9437184 | tf_op jit(solution)/shard_map/all_gather | solution.py:30
  10.2 254.0 %all-gather.13.cloned.1.call-start = ((), (), s32[]{:S(2)}) async-start(), calls=%async_computation.3 | async-start | bytes 9437184 | tf_op jit(solution)/shard_map/all_gather | solution.py:30
  188.8 168.1 %all-gather.11.cloned.1.call-start = ((), (), s32[]{:S(2)}) async-start(), calls=%async_computation.2 | async-start | bytes 17825792 | tf_op jit(solution)/shard_map/all_gather | solution.py:42
Sparse Core Ops, SparseCore 0:
  9.5 115.5 all-gather.6
  126.8 49.7 all-gather.8
  188.9 54.5 all-gather.12
  245.6 111.2 all-gather.10
where the time goes:
time: 393 us; the launch traced here: 392 us
  blocking collectives  139 us (35%)
  waiting for transfers between devices  128 us (33%)
  local copies, waits for them, and re-layouts  76.5 us (19%)
  matrix products  23.7 us (6%)
  between operations  14.5 us (4%)
  other arithmetic  10.5 us (3%)
    psum x2, blocking collectives, purify_section(): trace_now = lax.psum(diag_term, ('row', 'col'))  139 us
    all_gather x2, waiting for transfers between devices, purify_section(): lax.all_gather(panels, 'row', axis=1, tiled=True)  112 us
    gather x3, local copies, waits for them, and re-layouts, purify_section(): column_panels[position]  50.5 us
    dot_general x2, matrix products, purify_section(): jnp.einsum('ikuv,ilkvw->iluw', gathered_rows, picked, preferred_element_t...  23.7 us
    all_gather x2, waiting for transfers between devices, purify_section(): lax.all_gather(panels, 'col', axis=3, tiled=True)  15.1 us
    all_gather x1, local copies, waits for them, and re-layouts, purify_section(): lax.all_gather(panels, 'col', axis=3, tiled=True)  11.5 us
  transfers between devices with their start and end apart: 4, of which 3 were waited for; matrix products, arithmetic and copies ran while one was open for 17% of the time, Pallas kernels for 0%

commit v1 on v0

--- a/solution.py
+++ b/solution.py
@@ -4,6 +4,28 @@
 from jax.sharding import PartitionSpec as P
 
 ITERS = 2
+
+
+def joined_along(pieces, dim):
+    pieces = jnp.moveaxis(pieces, 0, dim)
+    shape = pieces.shape
+    return pieces.reshape(*shape[:dim], shape[dim] * shape[dim + 1], *shape[dim + 2 :])
+
+
+def gather_around(value, axis, dim):
+    devices = lax.axis_size(axis)
+    pairs = [(i, (i + 1) % devices) for i in range(devices)]
+    back = [(b, a) for a, b in pairs]
+    lower, upper = ([], [])
+    for step in range(devices - 1):
+        if step % 2 == 0:
+            lower.append(lax.ppermute(lower[-1] if lower else value, axis, pairs))
+        else:
+            upper.append(lax.ppermute(upper[-1] if upper else value, axis, back))
+    blocks = jnp.stack([*lower[::-1], value, *upper])
+    shift = lax.axis_index(axis) - len(lower)
+    blocks = blocks[(jnp.arange(devices) - shift) % devices]
+    return joined_along(blocks, dim)
 
 
 def purify_section(owned, cur_list, next_list, grid_rows, grid_cols, row_index, col_index):
@@ -27,7 +49,7 @@
     )
     next_trace = None
     trace_now = lax.psum(diag_term, ("row", "col"))
-    gathered_rows = lax.all_gather(panels, "col", axis=3, tiled=True).reshape(
+    gathered_rows = gather_around(panels, "col", 3).reshape(
         block_rows, slot_count, edge_size, edge_size
     )
     next_rows = lax.dynamic_index_in_dim(

time: 393 us -> 431 us (1.097)
  waiting for transfers between devices: 128 us -> 57.4 us
  local copies, waits for them, and re-layouts: 76.5 us -> 146 us
  starting transfers between devices: 0.12 us -> 24.3 us
  blocking collectives: 139 us -> 149 us
    all_gather x2, waiting for transfers between devices: 112 us -> 0.01 us  [purify_section(): lax.all_gather(panels, 'row', axis=1, tiled=True)]
    ppermute x0 -> x14, waiting for transfers between devices: none -> 57.3 us  [the longest x8 56.9 us: gather_around(): lower.append(lax.ppermute(lower[-1] if lower else value, axis, pairs))]
    unnamed x12 -> x27, local copies, waits for them, and re-layouts: 2.14 us -> 29.5 us
    ppermute x0 -> x14, starting transfers between devices: none -> 24.3 us  [the longest x8 18.6 us: gather_around(): lower.append(lax.ppermute(lower[-1] if lower else value, axis, pairs))]
    transpose x0 -> x2, local copies, waits for them, and re-layouts: none -> 19 us  [joined_along(): pieces = jnp.moveaxis(pieces, 0, dim)]
    gather x0 -> x2, local copies, waits for them, and re-layouts: none -> 16.1 us  [gather_around(): blocks = blocks[(jnp.arange(devices) - shift) % devices]]
    all_gather x2 -> x0, waiting for transfers between devices: 15.1 us -> none  [purify_section(): lax.all_gather(panels, 'col', axis=3, tiled=True)]
    psum x2, blocking collectives: 139 us -> 149 us  [purify_section(): trace_now = lax.psum(diag_term, ('row', 'col'))]
  transfers between devices with their start and end apart: 4 -> 16, of which waited for: 3 -> 7; matrix products, arithmetic and copies ran while one was open for 17% -> 21% of each run, Pallas kernels for 0% -> 0%
where the time goes in v1:
time: 431 us; the launch traced here: 429 us
  blocking collectives  149 us (35%)
  local copies, waits for them, and re-layouts  146 us (34%)
  waiting for transfers between devices  57.4 us (13%)
  starting transfers between devices  24.3 us (6%)
  matrix products  23.6 us (5%)
  between operations  14.8 us (3%)
  other arithmetic  13.2 us (3%)
    psum x2, blocking collectives, purify_section(): trace_now = lax.psum(diag_term, ('row', 'col'))  149 us
    ppermute x8, waiting for transfers between devices, gather_around(): lower.append(lax.ppermute(lower[-1] if lower else value, axis, pairs))  56.9 us
    gather x3, local copies, waits for them, and re-layouts, purify_section(): column_panels[position]  49.9 us
    unnamed x27, local copies, waits for them, and re-layouts  29.5 us
    dot_general x2, matrix products, purify_section(): jnp.einsum('ikuv,ilkvw->iluw', gathered_rows, picked, preferred_element_t...  23.6 us
    transpose x2, local copies, waits for them, and re-layouts, joined_along(): pieces = jnp.moveaxis(pieces, 0, dim)  19 us
    ppermute x8, starting transfers between devices, gather_around(): lower.append(lax.ppermute(lower[-1] if lower else value, axis, pairs))  18.6 us
    gather x2, local copies, waits for them, and re-layouts, gather_around(): blocks = blocks[(jnp.arange(devices) - shift) % devices]  16.1 us
  transfers between devices with their start and end apart: 16, of which 7 were waited for; matrix products, arithmetic and copies ran while one was open for 21% of the time, Pallas kernels for 0%

profile of v1, /device:TPU:1, one launch (start us, length us, event | category | flops | bytes accessed | tf_op | source)
XLA Modules:
  0.0 428.9 jit_solution(8795401166853029946)
XLA Ops:
  6.5 2.8 fusion.22
  11.2 3.0 collective-permute-start
  15.8 10.1 %collective-permute-done = bf16[4,1,2,1,256,256]{5,4,2,0,3,1:T(8,128)(2,1)} collective-permute-done((bf16[4,1,2,1,256,256]{5,4,2,0,3,1:T(8,128)(2,1)S(1)}, bf16[4,1,2,1,256,256]{5,4,2,0,3,1:T(8,128)(2,1)}, u32[]{:S(2)}, u32[]{:S(2)}) %collective-permute-start) | collective-permute-done | bytes 1048608 | tf_op jit(solution)/shard_map/ppermute | solution.py:22
  25.9 2.6 collective-permute-start.1
  31.4 9.2 %collective-permute-done.1 = bf16[4,1,2,1,256,256]{5,4,2,0,3,1:T(8,128)(2,1)} collective-permute-done((bf16[4,1,2,1,256,256]{5,4,2,0,3,1:T(8,128)(2,1)}, bf16[4,1,2,1,256,256]{5,4,2,0,3,1:T(8,128)(2,1)}, u32[]{:S(2)}, u32[]{:S(2)}) %collective-permute-start.1) | collective-permute-done | bytes 1048608 | tf_op jit(solution)/shard_map/ppermute | solution.py:22
  40.6 2.5 collective-permute-start.2
  50.2 4.9 %collective-permute-done.2 = bf16[4,1,2,1,256,256]{5,4,2,0,3,1:T(8,128)(2,1)} collective-permute-done((bf16[4,1,2,1,256,256]{5,4,2,0,3,1:T(8,128)(2,1)}, bf16[4,1,2,1,256,256]{5,4,2,0,3,1:T(8,128)(2,1)}, u32[]{:S(2)}, u32[]{:S(2)}) %collective-permute-start.2) | collective-permute-done | bytes 1048608 | tf_op jit(solution)/shard_map/ppermute | solution.py:22
  55.1 2.5 collective-permute-start.3
  57.6 76.3 %psum.14 = f32[]{:T(128)} all-reduce(f32[]{:T(128)} %select_reduce_fusion.6), channel_id=1, replica_groups=mesh['row'=16,'col'=8] {'row','col'}, use_global_device_ids=true, to_apply=%region_2.3 | all-reduce | flops 1 | bytes 8 | tf_op jit(solution)/shard_map/psum | solution.py:51
  136.0 2.9 copy.204
  143.1 2.3 bitcast_dynamic-update-slice_fusion.5
  151.1 2.3 bitcast_dynamic-update-slice_fusion.1
  155.5 8.0 %gather_fusion.2 = bf16[8,4,2,256,256]{4,3,2,1,0:T(8,128)(2,1)} fusion(bf16[8,4,2,256,256]{4,3,2,1,0:T(8,128)(2,1)} %bitcast.28, s32[1024]{0:T(1024)S(1)} %pad_clamp_fusion.2), kind=kCustom, calls=%fused_computation.2 | custom fusion | bytes 16777248 | tf_op jit(solution)/shard_map/gather | solution.py:27
  163.5 7.6 %copy.200 = bf16[4,1,2,8,1,256,256]{6,5,3,2,0,4,1:T(8,128)(2,1)} copy(bf16[4,1,2,8,1,256,256]{6,5,2,0,3,4,1:T(8,128)(2,1)} %bitcast.153) | data formatting | bytes 16777216 | tf_op jit(solution)/shard_map/transpose | solution.py:10
  171.1 13.9 %copy.190 = bf16[4,16,2,1,256,256]{5,4,2,1,0,3:T(8,128)(2,1)} copy(bf16[4,16,2,1,256,256]{5,4,3,2,0,1:T(8,128)(2,1)} %all-gather.4.cloned.1.call-done) | data formatting | bytes 33554432 | tf_op jit(solution)/shard_map/all_gather | solution.py:64
  185.0 14.2 %gather_fusion.1 = bf16[128,256,256]{2,1,0:T(8,128)(2,1)} fusion(bf16[128,256,256]{2,1,0:T(8,128)(2,1)} %bitcast.149, s32[1024]{0:T(1024)S(1)} %pad_clamp_fusion.3), kind=kCustom, calls=%fused_computation.1 | custom fusion | bytes 33554944 | tf_op jit(solution)/shard_map/gather | solution.py:80
  199.2 21.7 %copy.192 = bf16[4,2,16,256,256]{3,4,2,1,0:T(8,128)(2,1)} copy(bf16[4,2,16,256,256]{4,3,2,1,0:T(8,128)(2,1)} %bitcast.150) | data formatting | bytes 33554432 | tf_op jit(solution)/shard_map/gather | solution.py:80
  220.8 12.1 %select_reduce_fusion.2 = (f32[4,2]{1,0:T(4,128)S(1)}, bf16[4,2,256,256]{2,3,1,0:T(8,128)(2,1)}, f32[4,2,256,256]{2,3,1,0:T(8,128)}) fusion(pred[256,256]{0,1:T(8,128)(4,1)S(1)} %iota_compare_fusion, f32[4,2,256,256]{2,3,1,0:T(8,128)S(1)} %copy-done.2, bf16[4,16,256,256,1]{3,2,1,4,0:T(8,128)(2,1)} %bitcast.156, bf16[4,2,16,256,256]{3,4,2,1,0:T(8,128)(2,1)} %copy.192, ...), kind=kOutput, calls=%fused_computation.22 | convolution fusion | flops 4306501632 | bytes 30474400 | tf_op jit(solution)/shard_map/ikuv,ilkvw->iluw/dot_general | solution.py:82
  233.6 12.1 %collective-permute-done.7 = bf16[4,1,2,1,256,256]{4,5,2,0,3,1:T(8,128)(2,1)S(1)} collective-permute-done((bf16[4,1,2,1,256,256]{4,5,2,0,3,1:T(8,128)(2,1)}, bf16[4,1,2,1,256,256]{4,5,2,0,3,1:T(8,128)(2,1)S(1)}, u32[]{:S(2)}, u32[]{:S(2)}) %collective-permute-start.7) | collective-permute-done | bytes 1048608 | tf_op jit(solution)/shard_map/ppermute | solution.py:22
  245.6 2.4 collective-permute-start.8
  248.7 11.0 %collective-permute-done.8 = bf16[4,1,2,1,256,256]{4,5,2,0,3,1:T(8,128)(2,1)S(1)} collective-permute-done((bf16[4,1,2,1,256,256]{4,5,2,0,3,1:T(8,128)(2,1)S(1)}, bf16[4,1,2,1,256,256]{4,5,2,0,3,1:T(8,128)(2,1)S(1)}, u32[]{:S(2)}, u32[]{:S(2)}) %collective-permute-start.8) | collective-permute-done | bytes 1048608 | tf_op jit(solution)/shard_map/ppermute | solution.py:22
  259.7 2.5 collective-permute-start.9
  264.3 9.7 %collective-permute-done.9 = bf16[4,1,2,1,256,256]{4,5,2,0,3,1:T(8,128)(2,1)} collective-permute-done((bf16[4,1,2,1,256,256]{4,5,2,0,3,1:T(8,128)(2,1)S(1)}, bf16[4,1,2,1,256,256]{4,5,2,0,3,1:T(8,128)(2,1)}, u32[]{:S(2)}, u32[]{:S(2)}) %collective-permute-start.9) | collective-permute-done | bytes 1048608 | tf_op jit(solution)/shard_map/ppermute | solution.py:22
  274.0 2.6 collective-permute-start.10
  278.2 73.0 %psum.15 = f32[]{:T(128)} all-reduce(f32[]{:T(128)} %select_reduce_fusion.5), channel_id=1, replica_groups=mesh['row'=16,'col'=8] {'row','col'}, use_global_device_ids=true, to_apply=%region_8.9 | all-reduce | flops 1 | bytes 8 | tf_op jit(solution)/shard_map/psum | solution.py:51
  360.5 2.3 bitcast_dynamic-update-slice_fusion.13
  368.4 2.3 bitcast_dynamic-update-slice_fusion.9
  374.1 8.0 %gather_fusion.5 = bf16[8,4,2,256,256]{3,4,2,1,0:T(8,128)(2,1)} fusion(bf16[8,4,2,256,256]{3,4,2,1,0:T(8,128)(2,1)} %bitcast.58, s32[1024]{0:T(1024)S(1)} %pad_clamp_fusion.2), kind=kCustom, calls=%fused_computation.5 | custom fusion | bytes 16777248 | tf_op jit(solution)/shard_map/gather | solution.py:27
  382.1 11.5 %copy.212 = bf16[4,1,2,8,1,256,256]{6,5,3,2,0,4,1:T(8,128)(2,1)} copy(bf16[4,1,2,8,1,256,256]{5,6,2,0,3,4,1:T(8,128)(2,1)} %bitcast.152) | data formatting | bytes 16777216 | tf_op jit(solution)/shard_map/transpose | solution.py:10
  393.6 14.1 %gather_fusion.4 = bf16[128,256,256]{1,2,0:T(8,128)(2,1)} fusion(bf16[128,256,256]{1,2,0:T(8,128)(2,1)} %bitcast.154, s32[1024]{0:T(1024)S(1)} %pad_clamp_fusion), kind=kCustom, calls=%fused_computation.4 | custom fusion | bytes 33554944 | tf_op jit(solution)/shard_map/gather | solution.py:80
  407.6 11.6 %fusion.8 = f32[4,1,2,1,256,256]{4,5,2,0,3,1:T(8,128)} fusion(f32[4,2,256,256]{2,3,1,0:T(8,128)S(1)} %copy.216, bf16[4,16,256,256,1]{3,2,1,4,0:T(8,128)(2,1)} %bitcast.157, bf16[4,2,16,256,256]{3,4,2,1,0:T(8,128)(2,1)} %bitcast.155, pred[4,2,16]{2,1,0:T(4,128)(4,1)S(1)} %copy.210, pred[]{:T(512)S(6)} %gt.7), kind=kOutput, calls=%fused_computation.18 | convolution fusion | flops 4304928768 | bytes 29360256 | tf_op jit(solution)/shard_map/ikuv,ilkvw->iluw/dot_general | solution.py:82
  419.2 2.9 copy.217
  (104 shorter events, 49.5 us)
Async XLA Ops:
  6.5 36.5 %copy-start = (f32[4,1,2,1,256,256]{5,4,3,2,1,0:T(8,128)S(1)}, f32[4,1,2,1,256,256]{5,4,3,2,1,0:T(8,128)}, u32[]{:S(2)}) copy-start(f32[4,1,2,1,256,256]{5,4,3,2,1,0:T(8,128)} %param.7) | copy-start | bytes 6291460
  6.5 164.6 %all-gather.4.cloned.1.call-start = ((), (), s32[]{:S(2)}) async-start(), calls=%async_computation | async-start | bytes 17825792 | tf_op jit(solution)/shard_map/all_gather | solution.py:64
  9.4 384.2 %all-gather.6.cloned.1.call-start = ((), (), s32[]{:S(2)}) async-start(), calls=%async_computation.1 | async-start | bytes 17825792 | tf_op jit(solution)/shard_map/all_gather | solution.py:64
  11.2 14.8 %collective-permute-start = (bf16[4,1,2,1,256,256]{5,4,2,0,3,1:T(8,128)(2,1)S(1)}, bf16[4,1,2,1,256,256]{5,4,2,0,3,1:T(8,128)(2,1)}, u32[]{:S(2)}, u32[]{:S(2)}) collective-permute-start(bf16[4,1,2,1,256,256]{5,4,2,0,3,1:T(8,128)(2,1)S(1)} %bitcast_convert_fusion), channel_id=1, source_target_pairs={{0,1},{1,2},{2,3},{3,4},{4,5},{5,6},{6,7},{7,0},{8,9},{9,10},{10,1... | collective-permute-start | bytes 3145736 | tf_op jit(solution)/shard_map/ppermute | solution.py:22
  14.2 34.6 %collective-permute-start.4 = (bf16[4,1,2,1,256,256]{5,4,2,0,3,1:T(8,128)(2,1)S(1)}, bf16[4,1,2,1,256,256]{5,4,2,0,3,1:T(8,128)(2,1)}, u32[]{:S(2)}, u32[]{:S(2)}) collective-permute-start(bf16[4,1,2,1,256,256]{5,4,2,0,3,1:T(8,128)(2,1)S(1)} %bitcast_convert_fusion), channel_id=1, source_target_pairs={{1,0},{2,1},{3,2},{4,3},{5,4},{6,5},{7,6},{0,7},{9,8},{10,9},{11,1... | collective-permute-start | bytes 3145736 | tf_op jit(solution)/shard_map/ppermute | solution.py:24
  25.9 14.6 %collective-permute-start.1 = (bf16[4,1,2,1,256,256]{5,4,2,0,3,1:T(8,128)(2,1)}, bf16[4,1,2,1,256,256]{5,4,2,0,3,1:T(8,128)(2,1)}, u32[]{:S(2)}, u32[]{:S(2)}) collective-permute-start(bf16[4,1,2,1,256,256]{5,4,2,0,3,1:T(8,128)(2,1)} %collective-permute-done), channel_id=1, source_target_pairs={{0,1},{1,2},{2,3},{3,4},{4,5},{5,6},{6,7},{7,0},{8,9},{9,10},{10,1... | collective-permute-start | bytes 3145736 | tf_op jit(solution)/shard_map/ppermute | solution.py:22
  40.6 14.5 %collective-permute-start.2 = (bf16[4,1,2,1,256,256]{5,4,2,0,3,1:T(8,128)(2,1)}, bf16[4,1,2,1,256,256]{5,4,2,0,3,1:T(8,128)(2,1)}, u32[]{:S(2)}, u32[]{:S(2)}) collective-permute-start(bf16[4,1,2,1,256,256]{5,4,2,0,3,1:T(8,128)(2,1)} %collective-permute-done.1), channel_id=1, source_target_pairs={{0,1},{1,2},{2,3},{3,4},{4,5},{5,6},{6,7},{7,0},{8,9},{9,10},{10,1... | collective-permute-start | bytes 3145736 | tf_op jit(solution)/shard_map/ppermute | solution.py:22
  48.8 90.9 %collective-permute-start.5 = (bf16[4,1,2,1,256,256]{5,4,2,0,3,1:T(8,128)(2,1)}, bf16[4,1,2,1,256,256]{5,4,2,0,3,1:T(8,128)(2,1)S(1)}, u32[]{:S(2)}, u32[]{:S(2)}) collective-permute-start(bf16[4,1,2,1,256,256]{5,4,2,0,3,1:T(8,128)(2,1)} %collective-permute-done.4), channel_id=1, source_target_pairs={{1,0},{2,1},{3,2},{4,3},{5,4},{6,5},{7,6},{0,7},{9,8},{10,9},{11,1... | collective-permute-start | bytes 3145736 | tf_op jit(solution)/shard_map/ppermute | solution.py:24
  55.1 85.7 %collective-permute-start.3 = (bf16[4,1,2,1,256,256]{5,4,2,0,3,1:T(8,128)(2,1)}, bf16[4,1,2,1,256,256]{5,4,2,0,3,1:T(8,128)(2,1)}, u32[]{:S(2)}, u32[]{:S(2)}) collective-permute-start(bf16[4,1,2,1,256,256]{5,4,2,0,3,1:T(8,128)(2,1)} %collective-permute-done.2), channel_id=1, source_target_pairs={{0,1},{1,2},{2,3},{3,4},{4,5},{5,6},{6,7},{7,0},{8,9},{9,10},{10,1... | collective-permute-start | bytes 3145736 | tf_op jit(solution)/shard_map/ppermute | solution.py:22
  139.6 14.8 %collective-permute-start.6 = (bf16[4,1,2,1,256,256]{5,4,2,0,3,1:T(8,128)(2,1)S(1)}, bf16[4,1,2,1,256,256]{5,4,2,0,3,1:T(8,128)(2,1)S(1)}, u32[]{:S(2)}, u32[]{:S(2)}) collective-permute-start(bf16[4,1,2,1,256,256]{5,4,2,0,3,1:T(8,128)(2,1)S(1)} %collective-permute-done.5), channel_id=1, source_target_pairs={{1,0},{2,1},{3,2},{4,3},{5,4},{6,5},{7,6},{0,7},{9,8},{10,9},{11,1... | collective-permute-start | bytes 3145736 | tf_op jit(solution)/shard_map/ppermute | solution.py:24
  199.2 21.7 %copy-start.2 = (f32[4,2,256,256]{2,3,1,0:T(8,128)S(1)}, f32[4,2,256,256]{2,3,1,0:T(8,128)}, u32[]{:S(2)}) copy-start(f32[4,2,256,256]{2,3,1,0:T(8,128)} %copy.204) | copy-start | bytes 6291460
  233.0 12.7 %collective-permute-start.7 = (bf16[4,1,2,1,256,256]{4,5,2,0,3,1:T(8,128)(2,1)}, bf16[4,1,2,1,256,256]{4,5,2,0,3,1:T(8,128)(2,1)S(1)}, u32[]{:S(2)}, u32[]{:S(2)}) collective-permute-start(bf16[4,1,2,1,256,256]{4,5,2,0,3,1:T(8,128)(2,1)} %bitcast.158), channel_id=1, source_target_pairs={{0,1},{1,2},{2,3},{3,4},{4,5},{5,6},{6,7},{7,0},{8,9},{9,10},{10,1... | collective-permute-start | bytes 3145736 | tf_op jit(solution)/shard_map/ppermute | solution.py:22
  245.6 30.9 %copy-start.3 = (bf16[4,1,2,1,256,256]{4,5,2,0,3,1:T(8,128)(2,1)}, bf16[4,1,2,1,256,256]{4,5,2,0,3,1:T(8,128)(2,1)S(1)}, u32[]{:S(2)}) copy-start(bf16[4,1,2,1,256,256]{4,5,2,0,3,1:T(8,128)(2,1)S(1)} %collective-permute-done.7) | copy-start | bytes 3145732
  245.6 14.1 %collective-permute-start.8 = (bf16[4,1,2,1,256,256]{4,5,2,0,3,1:T(8,128)(2,1)S(1)}, bf16[4,1,2,1,256,256]{4,5,2,0,3,1:T(8,128)(2,1)S(1)}, u32[]{:S(2)}, u32[]{:S(2)}) collective-permute-start(bf16[4,1,2,1,256,256]{4,5,2,0,3,1:T(8,128)(2,1)S(1)} %collective-permute-done.7), channel_id=1, source_target_pairs={{0,1},{1,2},{2,3},{3,4},{4,5},{5,6},{6,7},{7,0},{8,9},{9,10},{10,1... | collective-permute-start | bytes 3145736 | tf_op jit(solution)/shard_map/ppermute | solution.py:22
  248.0 14.7 %collective-permute-start.11 = (bf16[4,1,2,1,256,256]{4,5,2,0,3,1:T(8,128)(2,1)}, bf16[4,1,2,1,256,256]{4,5,2,0,3,1:T(8,128)(2,1)}, u32[]{:S(2)}, u32[]{:S(2)}) collective-permute-start(bf16[4,1,2,1,256,256]{4,5,2,0,3,1:T(8,128)(2,1)} %bitcast.159), channel_id=1, source_target_pairs={{1,0},{2,1},{3,2},{4,3},{5,4},{6,5},{7,6},{0,7},{9,8},{10,9},{11,1... | collective-permute-start | bytes 3145736 | tf_op jit(solution)/shard_map/ppermute | solution.py:24
  259.7 92.1 %copy-start.4 = (bf16[4,1,2,1,256,256]{4,5,2,0,3,1:T(8,128)(2,1)}, bf16[4,1,2,1,256,256]{4,5,2,0,3,1:T(8,128)(2,1)S(1)}, u32[]{:S(2)}) copy-start(bf16[4,1,2,1,256,256]{4,5,2,0,3,1:T(8,128)(2,1)S(1)} %collective-permute-done.8) | copy-start | bytes 3145732
  259.7 14.2 %collective-permute-start.9 = (bf16[4,1,2,1,256,256]{4,5,2,0,3,1:T(8,128)(2,1)S(1)}, bf16[4,1,2,1,256,256]{4,5,2,0,3,1:T(8,128)(2,1)}, u32[]{:S(2)}, u32[]{:S(2)}) collective-permute-start(bf16[4,1,2,1,256,256]{4,5,2,0,3,1:T(8,128)(2,1)S(1)} %collective-permute-done.8), channel_id=1, source_target_pairs={{0,1},{1,2},{2,3},{3,4},{4,5},{5,6},{6,7},{7,0},{8,9},{9,10},{10,1... | collective-permute-start | bytes 3145736 | tf_op jit(solution)/shard_map/ppermute | solution.py:22
  262.7 94.7 %collective-permute-start.12 = (bf16[4,1,2,1,256,256]{4,5,2,0,3,1:T(8,128)(2,1)}, bf16[4,1,2,1,256,256]{4,5,2,0,3,1:T(8,128)(2,1)}, u32[]{:S(2)}, u32[]{:S(2)}) collective-permute-start(bf16[4,1,2,1,256,256]{4,5,2,0,3,1:T(8,128)(2,1)} %collective-permute-done.11), channel_id=1, source_target_pairs={{1,0},{2,1},{3,2},{4,3},{5,4},{6,5},{7,6},{0,7},{9,8},{10,9},{11,1... | collective-permute-start | bytes 3145736 | tf_op jit(solution)/shard_map/ppermute | solution.py:24
  274.0 84.2 %collective-permute-start.10 = (bf16[4,1,2,1,256,256]{4,5,2,0,3,1:T(8,128)(2,1)}, bf16[4,1,2,1,256,256]{4,5,2,0,3,1:T(8,128)(2,1)}, u32[]{:S(2)}, u32[]{:S(2)}) collective-permute-start(bf16[4,1,2,1,256,256]{4,5,2,0,3,1:T(8,128)(2,1)} %collective-permute-done.9), channel_id=1, source_target_pairs={{0,1},{1,2},{2,3},{3,4},{4,5},{5,6},{6,7},{7,0},{8,9},{9,10},{10,1... | collective-permute-start | bytes 3145736 | tf_op jit(solution)/shard_map/ppermute | solution.py:22
  353.8 13.6 %copy-start.1 = (bf16[4,2,256,256]{2,3,1,0:T(8,128)(2,1)S(1)}, bf16[4,2,256,256]{2,3,1,0:T(8,128)(2,1)}, u32[]{:S(2)}) copy-start(bf16[4,2,256,256]{2,3,1,0:T(8,128)(2,1)} %get-tuple-element.14) | copy-start | bytes 3145732
  357.4 15.6 %collective-permute-start.13 = (bf16[4,1,2,1,256,256]{4,5,2,0,3,1:T(8,128)(2,1)}, bf16[4,1,2,1,256,256]{4,5,2,0,3,1:T(8,128)(2,1)S(1)}, u32[]{:S(2)}, u32[]{:S(2)}) collective-permute-start(bf16[4,1,2,1,256,256]{4,5,2,0,3,1:T(8,128)(2,1)} %collective-permute-done.12), channel_id=1, source_target_pairs={{1,0},{2,1},{3,2},{4,3},{5,4},{6,5},{7,6},{0,7},{9,8},{10,9},{11,1... | collective-permute-start | bytes 3145736 | tf_op jit(solution)/shard_map/ppermute | solution.py:24
Sparse Core Ops, SparseCore 0:
  9.5 115.4 all-gather.3
  233.1 109.0 all-gather.5
